TPU v7x, 256 devices: a whole 4x4x8 slice. The times are simulated.
256 devices in a mesh: rows: 16 (over x, y), sub: 16 (over z, core).
Axes of the slice: x: 4, y: 4, z: 8, core: 2. Of those that a mesh axis runs over, the one named last changes fastest.
Arguments:
- embeddings: bfloat16 [65536, 1024], P(('rows', 'sub'))
- codes: int32 [64, 65536], P(None, ('rows', 'sub')), may hold values from 0 to 255
- codebook: bfloat16 [256, 1024], P(None, 'sub'), may hold values from -6 to 6
Outputs:
- rotation: float32 [1024, 1024], P('sub')
- rotated: bfloat16 [65536, 1024], P(('rows', 'sub'))
- new_codebook: float32 [256, 1024], P(None, 'sub')
All inputs are finite; a program needn't handle non-finite values.
Results may differ from a plain program's by a relative error of at most 0.0095.
Values may be sent and summed in bfloat16 or wider, within the bound.
No kernel may reach another device: no remote copies, remote signals or barrier semaphores. Data moves between devices by JAX's collectives and lax.ppermute only.
A program may use at most 64 MiB of HBM per device.

v0:
```python
import math
import jax
import jax.numpy as jnp
from jax import lax
from jax.sharding import PartitionSpec as P

NS_STEPS = 3
coef_a = 3.4445
coef_b = -4.775
coef_c = 2.0315
frob_eps = 1e-07


def one_hot_codes(code_block, count_codes):
    levels = lax.broadcasted_iota(jnp.int32, code_block.shape + (count_codes,), 2)
    return (code_block[:, :, None] == levels).astype(jnp.bfloat16)


def decode_rows(codes, table):
    subspaces, local_rows = codes.shape
    count_codes, row_width = table.shape
    sub_width = row_width // subspaces
    codewords = table.reshape(count_codes, subspaces, sub_width)
    one_hot = one_hot_codes(codes, count_codes)
    picked = jnp.einsum("mnk,kmj->nmj", one_hot, codewords, preferred_element_type=jnp.float32)
    return picked.reshape(local_rows, row_width).astype(jnp.bfloat16)


def codeword_totals(codes, row_values, count_codes):
    subspaces, local_rows = codes.shape
    row_width = row_values.shape[1]
    sub_width = row_width // subspaces
    one_hot = one_hot_codes(codes, count_codes)
    pieces = row_values.reshape(local_rows, subspaces, sub_width)
    code_sums = jnp.einsum("mnk,nmj->kmj", one_hot, pieces, preferred_element_type=jnp.float32)
    counts = jnp.sum(one_hot, axis=1, dtype=jnp.float32).T
    return (code_sums.reshape(count_codes, row_width), counts)


def bdot(left, right, dims):
    return lax.dot_general(
        left.astype(jnp.bfloat16),
        right.astype(jnp.bfloat16),
        (dims, ((), ())),
        preferred_element_type=jnp.float32,
    )


def newton_step(z):
    z_half = z.astype(jnp.bfloat16)
    gram = bdot(z_half, z_half, ((1,), (1,)))
    quartic = bdot(gram, gram, ((1,), (0,)))
    mixer = coef_b * gram + coef_c * quartic
    return coef_a * z + bdot(mixer, z_half, ((1,), (0,)))


def body(embeddings, codes, codebook):
    table = lax.all_gather(codebook, "sub", axis=1, tiled=True)
    decoded = decode_rows(codes, table)
    partial = lax.dot_general(
        embeddings, decoded, (((0,), (0,)), ((), ())), preferred_element_type=jnp.float32
    )
    cross = lax.psum(partial, ("rows", "sub"))
    frob_scale = jnp.sqrt(jnp.sum(cross * cross)) + frob_eps
    z = cross / frob_scale
    for newton_step_index in range(NS_STEPS):
        z = newton_step(z)
    rotation_half = z.astype(jnp.bfloat16)
    rotated = jnp.dot(embeddings, rotation_half, preferred_element_type=jnp.float32).astype(
        jnp.bfloat16
    )
    code_sums, counts = codeword_totals(codes, rotated, table.shape[0])
    code_sums = lax.psum(code_sums, ("rows", "sub"))
    counts = lax.psum(counts, ("rows", "sub"))
    me = lax.axis_index("sub")
    cols = codebook.shape[1]
    own_subspaces = counts.shape[1] * cols // code_sums.shape[1]
    own_sums = lax.dynamic_slice_in_dim(code_sums, me * cols, cols, axis=1)
    own_counts = lax.dynamic_slice_in_dim(counts, me * own_subspaces, own_subspaces, axis=1)
    own_codebook = codebook.astype(jnp.float32)
    spread = jnp.repeat(own_counts, cols // own_subspaces, axis=1)
    new_codebook = (own_sums + own_codebook) / (spread + 1.0)
    panel_rows = z.shape[0] // lax.axis_size("sub")
    panel = lax.dynamic_slice_in_dim(z, me * panel_rows, panel_rows, axis=0)
    return (panel, rotated, new_codebook)


def solution(mesh):
    in_specs = (P(("rows", "sub"), None), P(None, ("rows", "sub")), P(None, "sub"))
    out_specs = (P("sub", None), P(("rows", "sub"), None), P(None, "sub"))
    return jax.shard_map(body, mesh=mesh, in_specs=in_specs, out_specs=out_specs, check_vma=False)
```

profile of v0, /device:TPU:6, one launch (start us, length us, event | category | flops | bytes accessed | tf_op | source)
XLA Modules:
  0.0 650.9 jit_solution(6691471587485620089)
XLA Ops:
  7.2 0.0 all-reduce.4.cloned.1.call-start
  7.2 21.8 %all_gather.3 = bf16[256,1024]{0,1:T(8,128)(2,1)S(1)} all-gather(bf16[256,64]{0,1:T(8,128)(2,1)} %param.5), channel_id=1, replica_groups=mesh['rows'=16,'sub'=16] {'sub'}, dimensions={1}, use_global_device_ids=true | all-gather | bytes 557056 | tf_op jit(solution)/shard_map/all_gather | solution.py:58
  29.0 5.3 fusion.14
  34.3 2.7 convolution_bitcast_fusion
  36.9 0.0 all-reduce.4.cloned.1.call-update
  37.0 0.0 all-reduce.6.cloned.1.call-start
  37.0 0.8 copy-done.2
  37.8 3.4 convert_reduce_fusion
  41.2 264.1 %all-reduce.4.cloned.1.call-done = f32[1024,1024]{0,1:T(8,128)} async-done(((f32[1024,1024]{0,1:T(8,128)}), f32[1024,1024]{0,1:T(8,128)}) %all-reduce.4.cloned.1.call-update) | async-done | bytes 4194320 | tf_op jit(solution)/shard_map/psum | solution.py:63
  305.3 3.9 multiply_reduce_fusion
  309.9 7.8 %fusion.28 = f32[1024,1024]{1,0:T(8,128)} fusion(f32[1024,1024]{0,1:T(8,128)} %all-reduce.4.cloned.1.call-done, f32[]{:T(128)S(6)} %add.47), kind=kOutput, calls=%fused_computation.30 | convolution fusion | flops 2149580800 | bytes 8388612 | tf_op jit(solution)/shard_map/dot_general | solution.py:41
  317.7 13.9 %multiply_add_fusion.2 = f32[1024,1024]{0,1:T(8,128)} fusion(f32[1024,1024]{0,1:T(8,128)} %all-reduce.4.cloned.1.call-done, f32[]{:T(128)S(6)} %add.47, f32[1024,1024]{1,0:T(8,128)} %fusion.28), kind=kOutput, calls=%fused_computation.12 | convolution fusion | flops 4305453056 | bytes 12582916 | tf_op jit(solution)/shard_map/dot_general | solution.py:41
  331.6 7.8 %fusion.21 = f32[1024,1024]{1,0:T(8,128)} fusion(f32[1024,1024]{0,1:T(8,128)} %multiply_add_fusion.2), kind=kOutput, calls=%fused_computation.28 | convolution fusion | flops 2148532224 | bytes 8388608 | tf_op jit(solution)/shard_map/dot_general | solution.py:41
  339.4 13.7 %multiply_add_fusion.1 = f32[1024,1024]{0,1:T(8,128)} fusion(f32[1024,1024]{0,1:T(8,128)} %multiply_add_fusion.2, f32[1024,1024]{1,0:T(8,128)} %fusion.21), kind=kOutput, calls=%fused_computation.10 | convolution fusion | flops 4303355904 | bytes 12582912 | tf_op jit(solution)/shard_map/dot_general | solution.py:41
  353.1 8.0 %fusion.18 = f32[1024,1024]{1,0:T(8,128)} fusion(f32[1024,1024]{0,1:T(8,128)} %multiply_add_fusion.1), kind=kOutput, calls=%fused_computation.25 | convolution fusion | flops 2148532224 | bytes 8388608 | tf_op jit(solution)/shard_map/dot_general | solution.py:41
  361.2 13.9 %multiply_add_fusion = f32[1024,1024]{0,1:T(8,128)} fusion(f32[1024,1024]{0,1:T(8,128)} %multiply_add_fusion.1, f32[1024,1024]{1,0:T(8,128)} %fusion.18), kind=kOutput, calls=%fused_computation.8 | convolution fusion | flops 4303355904 | bytes 12582912 | tf_op jit(solution)/shard_map/dot_general | solution.py:41
  375.1 2.9 fusion.11
  378.0 5.1 fusion.1
  383.1 1.2 constant_dynamic-slice_fusion
  384.4 0.9 copy.9
  385.3 1.0 copy.10
  386.3 255.6 %all-reduce.6.cloned.1.call-done = (f32[256,1024]{0,1:T(8,128)}, f32[256,64]{0,1:T(8,128)}) async-done(((f32[256,1024]{0,1:T(8,128)}, f32[256,64]{0,1:T(8,128)}), (f32[256,1024]{0,1:T(8,128)}, f32[256,64]{0,1:T(8,128)})) %all-reduce.6.cloned.1.call-update) | async-done | bytes 1114128 | tf_op jit(solution)/shard_map/psum | solution.py:73
  641.9 0.7 dynamic-slice_add_fusion
  642.6 1.5 bitcast_divide_fusion
  (6 shorter events, 0.0 us)
Async XLA Ops:
  7.2 27.1 %copy-start = (bf16[256,1024]{1,0:T(8,128)(2,1)S(1)}, bf16[256,1024]{1,0:T(8,128)(2,1)}, u32[]{:S(2)}) copy-start(bf16[256,1024]{1,0:T(8,128)(2,1)} %param.3) | copy-start | bytes 1572868
  7.2 298.1 %all-reduce.4.cloned.1.call-start = ((), (), s32[]{:S(2)}) async-start(), calls=%async_computation | async-start | bytes 8388608 | tf_op jit(solution)/shard_map/psum | solution.py:63
  36.9 0.8 copy-start.2
  37.0 604.9 %all-reduce.6.cloned.1.call-start = ((), (), s32[]{:S(2)}) async-start(), calls=%async_computation.1 | async-start | bytes 2228224 | tf_op jit(solution)/shard_map/psum | solution.py:73
  378.0 264.6 %copy-start.1 = (bf16[256,64]{0,1:T(8,128)(2,1)S(1)}, bf16[256,64]{0,1:T(8,128)(2,1)}, u32[]{:S(2)}) copy-start(bf16[256,64]{0,1:T(8,128)(2,1)} %param.5) | copy-start | bytes 98308
Sparse Core Ops, SparseCore 0:
  37.1 268.1 all-reduce.3
  383.3 258.5 all-reduce.5
where the time goes:
time: 652 us; the launch traced here: 651 us
  waiting for transfers between devices  520 us (80%)
  matrix products  81.1 us (12%)
  blocking collectives  21.8 us (3%)
  between operations  14.8 us (2%)
  other arithmetic  9.48 us (1%)
    psum x1, waiting for transfers between devices, body(): cross = lax.psum(partial, ('rows', 'sub'))  264 us
    psum x1, waiting for transfers between devices, body(): code_sums = lax.psum(code_sums, ('rows', 'sub'))  256 us
    dot_general x6, matrix products, bdot(): lax.dot_general(left.astype(jnp.bfloat16), right.astype(jnp.bfloat16), (d...  65.2 us
    all_gather x1, blocking collectives, body(): table = lax.all_gather(codebook, 'sub', axis=1, tiled=True)  21.8 us
  transfers between devices with their start and end apart: 2, of which 2 were waited for; matrix products, arithmetic and copies ran while one was open for 1% of the time, Pallas kernels for 0%

commit v1 on v0

--- a/solution.py
+++ b/solution.py
@@ -55,7 +55,13 @@
 
 
 def body(embeddings, codes, codebook):
-    table = lax.all_gather(codebook, "sub", axis=1, tiled=True)
+    _end_domain = lambda point: jnp.concatenate(
+        jax.lax.all_to_all(
+            jnp.stack([point for _ in range(jax.lax.axis_size("sub"))]), "sub", 0, 0
+        ),
+        1,
+    )
+    table = _end_domain(codebook)
     decoded = decode_rows(codes, table)
     partial = lax.dot_general(
         embeddings, decoded, (((0,), (0,)), ((), ())), preferred_element_type=jnp.float32

time: 652 us -> 655 us (level)
    all_to_all x0 -> x1, blocking collectives: none -> 24.3 us  [body(): jax.lax.all_to_all(jnp.stack([point for _ in range(jax.lax.axis_size('sub...]
    all_gather x1 -> x0, blocking collectives: 21.8 us -> none  [body(): table = lax.all_gather(codebook, 'sub', axis=1, tiled=True)]
where the time goes in v1:
time: 655 us
  waiting for transfers between devices  520 us (79%)
  matrix products  81.1 us (12%)
  blocking collectives  24.3 us (4%)
  between operations  14.8 us (2%)
  other arithmetic  9.48 us (1%)
    psum x1, waiting for transfers between devices, body(): cross = lax.psum(partial, ('rows', 'sub'))  265 us
    psum x1, waiting for transfers between devices, body(): code_sums = lax.psum(code_sums, ('rows', 'sub'))  255 us
    dot_general x6, matrix products, bdot(): lax.dot_general(left.astype(jnp.bfloat16), right.astype(jnp.bfloat16), (d...  65.2 us
    all_to_all x1, blocking collectives, body(): jax.lax.all_to_all(jnp.stack([point for _ in range(jax.lax.axis_size('sub...  24.3 us
  transfers between devices with their start and end apart: 2, of which 2 were waited for; matrix products, arithmetic and copies ran while one was open for 1% of the time, Pallas kernels for 0%

profile of v1, /device:TPU:6, one launch (start us, length us, event | category | flops | bytes accessed | tf_op | source)
XLA Modules:
  0.0 654.6 jit_solution(3827931222654374977)
XLA Ops:
  7.2 0.0 all-reduce.4.cloned.1.call-start
  7.2 0.9 stack.2
  8.1 24.3 %all_to_all.5 = bf16[16,256,64]{1,2,0:T(8,128)(2,1)S(1)} all-to-all(bf16[16,256,64]{1,2,0:T(8,128)(2,1)S(1)} %stack.2), channel_id=1, replica_groups=mesh['rows'=16,'sub'=16] {'sub'}, dimensions={0} | all-to-all | bytes 1048576 | tf_op jit(solution)/shard_map/all_to_all | solution.py:59
  32.4 5.3 fusion.14
  37.7 2.7 convolution_bitcast_fusion
  40.3 0.0 all-reduce.6.cloned.1.call-start
  40.4 0.8 copy-done.2
  41.1 3.4 convert_reduce_fusion
  44.6 264.6 %all-reduce.4.cloned.1.call-done = f32[1024,1024]{0,1:T(8,128)} async-done(((f32[1024,1024]{0,1:T(8,128)}), f32[1024,1024]{0,1:T(8,128)}) %all-reduce.4.cloned.1.call-update) | async-done | bytes 4194320 | tf_op jit(solution)/shard_map/psum | solution.py:69
  309.2 3.9 multiply_reduce_fusion
  313.8 7.8 %fusion.28 = f32[1024,1024]{1,0:T(8,128)} fusion(f32[1024,1024]{0,1:T(8,128)} %all-reduce.4.cloned.1.call-done, f32[]{:T(128)S(6)} %add.47), kind=kOutput, calls=%fused_computation.30 | convolution fusion | flops 2149580800 | bytes 8388612 | tf_op jit(solution)/shard_map/dot_general | solution.py:41
  321.6 13.9 %multiply_add_fusion.2 = f32[1024,1024]{0,1:T(8,128)} fusion(f32[1024,1024]{0,1:T(8,128)} %all-reduce.4.cloned.1.call-done, f32[]{:T(128)S(6)} %add.47, f32[1024,1024]{1,0:T(8,128)} %fusion.28), kind=kOutput, calls=%fused_computation.12 | convolution fusion | flops 4305453056 | bytes 12582916 | tf_op jit(solution)/shard_map/dot_general | solution.py:41
  335.5 7.8 %fusion.21 = f32[1024,1024]{1,0:T(8,128)} fusion(f32[1024,1024]{0,1:T(8,128)} %multiply_add_fusion.2), kind=kOutput, calls=%fused_computation.28 | convolution fusion | flops 2148532224 | bytes 8388608 | tf_op jit(solution)/shard_map/dot_general | solution.py:41
  343.3 13.7 %multiply_add_fusion.1 = f32[1024,1024]{0,1:T(8,128)} fusion(f32[1024,1024]{0,1:T(8,128)} %multiply_add_fusion.2, f32[1024,1024]{1,0:T(8,128)} %fusion.21), kind=kOutput, calls=%fused_computation.10 | convolution fusion | flops 4303355904 | bytes 12582912 | tf_op jit(solution)/shard_map/dot_general | solution.py:41
  357.0 8.0 %fusion.18 = f32[1024,1024]{1,0:T(8,128)} fusion(f32[1024,1024]{0,1:T(8,128)} %multiply_add_fusion.1), kind=kOutput, calls=%fused_computation.25 | convolution fusion | flops 2148532224 | bytes 8388608 | tf_op jit(solution)/shard_map/dot_general | solution.py:41
  365.1 13.9 %multiply_add_fusion = f32[1024,1024]{0,1:T(8,128)} fusion(f32[1024,1024]{0,1:T(8,128)} %multiply_add_fusion.1, f32[1024,1024]{1,0:T(8,128)} %fusion.18), kind=kOutput, calls=%fused_computation.8 | convolution fusion | flops 4303355904 | bytes 12582912 | tf_op jit(solution)/shard_map/dot_general | solution.py:41
  379.0 2.9 fusion.11
  381.9 5.1 fusion.1
  387.0 1.2 constant_dynamic-slice_fusion
  388.3 0.9 copy.9
  389.2 1.0 copy.10
  390.2 255.4 %all-reduce.6.cloned.1.call-done = (f32[256,1024]{0,1:T(8,128)}, f32[256,64]{0,1:T(8,128)}) async-done(((f32[256,1024]{0,1:T(8,128)}, f32[256,64]{0,1:T(8,128)}), (f32[256,1024]{0,1:T(8,128)}, f32[256,64]{0,1:T(8,128)})) %all-reduce.6.cloned.1.call-update) | async-done | bytes 1114128 | tf_op jit(solution)/shard_map/psum | solution.py:79
  645.6 0.7 dynamic-slice_add_fusion
  646.3 1.5 bitcast_divide_fusion
  (7 shorter events, 0.1 us)
Async XLA Ops:
  7.2 30.5 %copy-start = (bf16[256,1024]{1,0:T(8,128)(2,1)S(1)}, bf16[256,1024]{1,0:T(8,128)(2,1)}, u32[]{:S(2)}) copy-start(bf16[256,1024]{1,0:T(8,128)(2,1)} %param.3) | copy-start | bytes 1572868
  7.2 302.0 %all-reduce.4.cloned.1.call-start = ((), (), s32[]{:S(2)}) async-start(), calls=%async_computation.1 | async-start | bytes 8388608 | tf_op jit(solution)/shard_map/psum | solution.py:69
  40.3 0.8 copy-start.2
  40.3 605.3 %all-reduce.6.cloned.1.call-start = ((), (), s32[]{:S(2)}) async-start(), calls=%async_computation.2 | async-start | bytes 2228224 | tf_op jit(solution)/shard_map/psum | solution.py:79
  381.9 264.4 %copy-start.1 = (bf16[256,64]{0,1:T(8,128)(2,1)S(1)}, bf16[256,64]{0,1:T(8,128)(2,1)}, u32[]{:S(2)}) copy-start(bf16[256,64]{0,1:T(8,128)(2,1)} %param.5) | copy-start | bytes 98308
Sparse Core Ops, SparseCore 0:
  40.5 268.7 all-reduce.3
  387.1 258.4 all-reduce.5
